TPU v7x, 128 devices: a whole 4x4x4 slice. The times are simulated.
128 devices in a mesh: col: 8 (over z, core), grp: 16 (over x, y).
Axes of the slice: x: 4, y: 4, z: 4, core: 2. Of those that a mesh axis runs over, the one named last changes fastest.
Arguments:
- factor_rows: float32 [1024, 4, 8, 512], P('grp', None, 'col'), may hold values from -3 to 3, as said below
- new_rows: float32 [8192, 4, 8, 512], P('grp', None, 'col'), may hold values from -0.3125 to 0.3125
Outputs:
- updated_rows: float32 [1024, 4, 8, 512], P('grp', None, 'col')
Inputs may be any that keep to these rules, and one draw needn't show every extreme that they name: factor_rows is upper triangular in the global row and column numbers, with diagonal entries between 1 and 3.
All inputs are finite; a program needn't handle non-finite values.
Results may differ from a plain program's by a relative error of at most 0.00008.
Values sent between devices are 32-bit elements; how exact they have to be, the bound alone decides.
No kernel may reach another device: no remote copies, remote signals or barrier semaphores. Data moves between devices by JAX's collectives and lax.ppermute only.
A program may use at most 128 MiB of HBM per device.

v0:
```python
import jax
import jax.numpy as jnp
from jax import lax
from jax.sharding import PartitionSpec as P


def from_root(value, axis, source):
    kept = jnp.where(lax.axis_index(axis) == source, value, 0).astype(value.dtype)
    return lax.psum(kept, axis)


def solve_lower(lower, right):
    return lax.linalg.triangular_solve(lower, right, left_side=True, lower=True)


def shards(factor_rows, new_rows):
    highest = lax.Precision.HIGHEST
    own_rows = factor_rows.shape[0]
    npanel = factor_rows.shape[1]
    width = factor_rows.shape[3]
    local = jnp.concatenate([factor_rows, new_rows], 0).reshape(-1, npanel * width)
    panel = local[:, :width]
    first = from_root(panel, "col", 0)
    second = from_root(panel, "col", 1)
    part_one = jnp.dot(first.T, local, precision=highest, preferred_element_type=jnp.float32)
    part_two = jnp.dot(second.T, local, precision=highest, preferred_element_type=jnp.float32)
    both = jnp.concatenate([first, second], 1)
    small_one = jnp.dot(first.T, both, precision=highest, preferred_element_type=jnp.float32)
    small_two = jnp.dot(second.T, second, precision=highest, preferred_element_type=jnp.float32)
    gram_one, gram_two, corner_one, corner_two = lax.psum(
        (part_one, part_two, small_one, small_two), "grp"
    )
    lower_one = jnp.linalg.cholesky(corner_one[:, :width])
    cross = solve_lower(lower_one, corner_one[:, width:])
    lower_two = jnp.linalg.cholesky(corner_two - jnp.dot(cross.T, cross, precision=highest))
    upper_one = solve_lower(lower_one, gram_one)
    upper_two = solve_lower(lower_two, gram_two - jnp.dot(cross.T, upper_one, precision=highest))
    stacked = jnp.concatenate([upper_one, upper_two], 0)
    mine = lax.dynamic_slice_in_dim(stacked, lax.axis_index("grp") * own_rows, own_rows, 0)
    return mine.reshape(own_rows, npanel, 1, width)


def solution(mesh):
    placed = (P("grp", None, "col", None), P("grp", None, "col", None))
    return jax.shard_map(
        shards, mesh=mesh, in_specs=placed, out_specs=P("grp", None, "col", None), check_vma=False
    )
```

profile of v0, /device:TPU:1, one launch (start us, length us, event | category | flops | bytes accessed | tf_op | source)
XLA Modules:
  0.0 635.1 jit_solution(15138732121004060162)
XLA Ops:
  6.5 15.4 %maximum_reduce_fusion = f32[576,4,512]{2,1,0:T(4,128)S(1)} fusion(f32[512,4,1,512]{3,2,1,0:T(1,128)} %param.6, f32[64,4,1,512]{3,2,1,0:T(1,128)} %param.5), kind=kLoop, calls=%fused_computation.12 | loop fusion | flops 1179648 | bytes 9437184 | tf_op jit(solution)/shard_map/concatenate | solution.py:21
  22.0 4.3 copy.11
  26.3 3.1 slice_select_fusion.1
  29.9 68.0 %all-reduce.8.cloned.1.call-done = (f32[576,512]{1,0:T(8,128)}, f32[576,512]{1,0:T(8,128)}) async-done(((f32[576,512]{1,0:T(8,128)}, f32[576,512]{1,0:T(8,128)}), (f32[576,512]{1,0:T(8,128)}, f32[576,512]{1,0:T(8,128)})) %all-reduce.8.cloned.1.call-update) | async-done | bytes 2359312 | tf_op jit(solution)/shard_map/psum | solution.py:9
  97.9 13.7 %fusion.115 = f32[512,2048]{1,0:T(8,128)} fusion(f32[576,512]{1,0:T(8,128)} %get-tuple-element.51, f32[576,2048]{1,0:T(8,128)} %bitcast.121), kind=kOutput, calls=%fused_computation.189 | convolution fusion | flops 7247757312 | bytes 10092544 | tf_op jit(solution)/shard_map/dot_general | solution.py:26
  111.7 6.5 %fusion.29 = f32[512,1024]{0,1:T(8,128)} fusion(f32[576,512]{1,0:T(8,128)S(1)} %copy-done.1, f32[576,512]{1,0:T(8,128)S(1)} %copy-done), kind=kOutput, calls=%fused_computation.40 | convolution fusion | flops 3624468480 | bytes 4456448 | tf_op jit(solution)/shard_map/dot_general | solution.py:28
  118.2 11.9 %fusion.113 = f32[512,2048]{1,0:T(8,128)} fusion(f32[576,512]{1,0:T(8,128)S(1)} %copy-done.1, f32[576,2048]{1,0:T(8,128)S(1)} %bitcast.124), kind=kOutput, calls=%fused_computation.187 | convolution fusion | flops 7247757312 | bytes 10092544 | tf_op jit(solution)/shard_map/dot_general | solution.py:25
  130.0 3.8 fusion.114
  133.8 169.6 %all-reduce.6.cloned.1.call-done = (f32[512,2048]{1,0:T(8,128)}, f32[512,2048]{1,0:T(8,128)}, f32[512,1024]{0,1:T(8,128)}, f32[512,512]{0,1:T(8,128)}) async-done(((f32[512,2048]{1,0:T(8,128)}, f32[512,2048]{1,0:T(8,128)}, f32[512,1024]{0,1:T(8,128)}, f32[512,512]{0,1:T(8,128)}), (f32[512,2048]{1,0:T(8,128)}, f32[512,2048]{1,0:T(8,128)}, f32[512,1024]{0,1:T(8,128)}, ...) | async-done | bytes 11534352 | tf_op jit(solution)/shard_map/psum | solution.py:30
  303.4 2.4 slice.184
  305.8 1.6 copy.4
  308.7 11.7 %cholesky.286 = f32[128,128]{1,0:T(8,128)S(1)} custom-call(f32[128,128]{1,0:T(8,128)S(1)} %cholesky.426), custom_call_target="Cholesky" | custom-call | tf_op jit(solution)/shard_map/jit(cholesky)/cholesky | solution.py:33
  320.6 9.8 %custom-call.31 = f32[1,128,128]{1,2,0:T(8,128)S(1)} custom-call(f32[1,128,128]{2,1,0:T(8,128)S(1)} %get-tuple-element.78), custom_call_target="InvertDiagBlocksLowerTriangular" | custom-call | tf_op jit(solution)/shard_map/jit(cholesky)/cholesky | solution.py:33
  332.9 12.1 %cholesky.305 = f32[128,128]{1,0:T(8,128)S(1)} custom-call(f32[128,128]{1,0:T(8,128)S(1)} %cholesky.430), custom_call_target="Cholesky" | custom-call | tf_op jit(solution)/shard_map/jit(cholesky)/cholesky | solution.py:33
  345.0 9.8 %custom-call.32 = f32[1,128,128]{1,2,0:T(8,128)S(1)} custom-call(f32[1,128,128]{2,1,0:T(8,128)S(1)} %get-tuple-element.75), custom_call_target="InvertDiagBlocksLowerTriangular" | custom-call | tf_op jit(solution)/shard_map/jit(cholesky)/cholesky | solution.py:33
  356.4 11.7 %cholesky.326 = f32[128,128]{1,0:T(8,128)S(1)} custom-call(f32[128,128]{1,0:T(8,128)S(1)} %cholesky.435), custom_call_target="Cholesky" | custom-call | tf_op jit(solution)/shard_map/jit(cholesky)/cholesky | solution.py:33
  368.9 9.8 %custom-call.33 = f32[1,128,128]{1,2,0:T(8,128)S(1)} custom-call(f32[1,128,128]{2,1,0:T(8,128)S(1)} %get-tuple-element.72), custom_call_target="InvertDiagBlocksLowerTriangular" | custom-call | tf_op jit(solution)/shard_map/jit(cholesky)/cholesky | solution.py:33
  380.1 11.9 %cholesky.343 = f32[128,128]{1,0:T(8,128)S(1)} custom-call(f32[128,128]{1,0:T(8,128)S(1)} %convolution_subtract_fusion.13), custom_call_target="Cholesky" | custom-call | tf_op jit(solution)/shard_map/jit(cholesky)/cholesky | solution.py:33
  397.2 11.7 %while.5 = (s32[]{:T(128)}, f32[512,512]{1,0:T(8,128)}, s32[4,2]{0,1:T(2,128)S(1)}, f32[4,128,128]{2,1,0:T(8,128)S(1)}, s32[]{:T(128)}) while((s32[]{:T(128)}, f32[512,512]{1,0:T(8,128)}, s32[4,2]{0,1:T(2,128)S(1)}, f32[4,128,128]{2,1,0:T(8,128)S(1)}, s32[]{:T(128)}) %tuple.55), condition=%wide.while_cond, body=%wide.while_body.sunk | while | flops 2 | bytes 131181 | solution.py:13
  397.8 2.3 bitcast_dynamic-update-slice_fusion.4
  400.8 2.3 bitcast_dynamic-update-slice_fusion.4
  403.7 2.3 bitcast_dynamic-update-slice_fusion.4
  406.7 2.2 bitcast_dynamic-update-slice_fusion.4
  408.9 39.3 %custom-call.34 = f32[4,128,128]{1,2,0:T(8,128)S(1)} custom-call(f32[4,128,128]{2,1,0:T(8,128)S(1)} %get-tuple-element.29), custom_call_target="InvertDiagBlocksLowerTriangular" | custom-call | tf_op jit(solution)/shard_map/triangular_solve/custom-call.3 | solution.py:13
  448.7 1.4 convolution_subtract_fusion.6
  450.5 1.9 convolution_subtract_fusion.5
  452.9 2.4 convolution_subtract_fusion.7
  455.7 3.1 convolution_subtract_fusion.4
  460.4 11.7 %cholesky.358 = f32[128,128]{1,0:T(8,128)S(1)} custom-call(f32[128,128]{1,0:T(8,128)S(1)} %cholesky.439), custom_call_target="Cholesky" | custom-call | tf_op jit(solution)/shard_map/jit(cholesky)/cholesky | solution.py:35
  472.2 10.2 %custom-call.35 = f32[1,128,128]{1,2,0:T(8,128)S(1)} custom-call(f32[1,128,128]{2,1,0:T(8,128)S(1)} %get-tuple-element.68), custom_call_target="InvertDiagBlocksLowerTriangular" | custom-call | tf_op jit(solution)/shard_map/jit(cholesky)/cholesky | solution.py:35
  484.9 11.7 %cholesky.377 = f32[128,128]{1,0:T(8,128)S(1)} custom-call(f32[128,128]{1,0:T(8,128)S(1)} %cholesky.443), custom_call_target="Cholesky" | custom-call | tf_op jit(solution)/shard_map/jit(cholesky)/cholesky | solution.py:35
  498.0 9.8 %custom-call.36 = f32[1,128,128]{1,2,0:T(8,128)S(1)} custom-call(f32[1,128,128]{2,1,0:T(8,128)S(1)} %get-tuple-element.65), custom_call_target="InvertDiagBlocksLowerTriangular" | custom-call | tf_op jit(solution)/shard_map/jit(cholesky)/cholesky | solution.py:35
  509.4 11.7 %cholesky.398 = f32[128,128]{1,0:T(8,128)S(1)} custom-call(f32[128,128]{1,0:T(8,128)S(1)} %cholesky.448), custom_call_target="Cholesky" | custom-call | tf_op jit(solution)/shard_map/jit(cholesky)/cholesky | solution.py:35
  521.8 10.0 %custom-call.37 = f32[1,128,128]{1,2,0:T(8,128)S(1)} custom-call(f32[1,128,128]{2,1,0:T(8,128)S(1)} %get-tuple-element.62), custom_call_target="InvertDiagBlocksLowerTriangular" | custom-call | tf_op jit(solution)/shard_map/jit(cholesky)/cholesky | solution.py:35
  533.2 11.7 %cholesky.415 = f32[128,128]{1,0:T(8,128)S(1)} custom-call(f32[128,128]{1,0:T(8,128)S(1)} %convolution_subtract_fusion.12), custom_call_target="Cholesky" | custom-call | tf_op jit(solution)/shard_map/jit(cholesky)/cholesky | solution.py:35
  548.4 8.3 %while.6 = (s32[]{:T(128)}, f32[512,512]{1,0:T(8,128)S(1)}, s32[4,2]{0,1:T(2,128)S(1)}, f32[4,128,128]{2,1,0:T(8,128)S(1)}, s32[]{:T(128)}) while((s32[]{:T(128)}, f32[512,512]{1,0:T(8,128)S(1)}, s32[4,2]{0,1:T(2,128)S(1)}, f32[4,128,128]{2,1,0:T(8,128)S(1)}, s32[]{:T(128)}) %tuple.67), condition=%wide.while_cond.clone, body=%wide.while_body.clone.sunk | while | flops 2 | bytes 131181 | solution.py:13
  549.0 1.4 bitcast_dynamic-update-slice_fusion.5
  551.1 1.4 bitcast_dynamic-update-slice_fusion.5
  553.2 1.4 bitcast_dynamic-update-slice_fusion.5
  555.3 1.4 bitcast_dynamic-update-slice_fusion.5
  556.7 39.5 %custom-call.38 = f32[4,128,128]{1,2,0:T(8,128)S(1)} custom-call(f32[4,128,128]{2,1,0:T(8,128)S(1)} %get-tuple-element.30), custom_call_target="InvertDiagBlocksLowerTriangular" | custom-call | tf_op jit(solution)/shard_map/triangular_solve/custom-call.3 | solution.py:13
  596.2 2.3 fusion.41
  598.5 2.4 convolution_subtract_fusion.3
  602.0 2.2 convolution_subtract_fusion.1
  605.3 3.1 fusion.26
  609.5 7.8 %fusion.20 = f32[512,2048]{1,0:T(8,128)S(1)} fusion(f32[512,2048]{1,0:T(8,128)S(1)} %copy-done.3, f32[128,2048]{1,0:T(8,128)S(1)} %fusion.99, f32[128,2048]{1,0:T(8,128)S(1)} %fusion.97, f32[128,2048]{1,0:T(8,128)S(1)} %fusion.95, f32[128,2048]{1,0:T(8,128)S(1)} %fusion.41, f32[128,512]{1,0:T(8,128)S(1)} %fusion.98, f32[128,512]{1,0:T(8,128)S(1)} %fusion.96, ...), kind=kOutput, calls=%fused_computation.33 | convolution fusion | flops 6447431680 | bytes 13631488 | tf_op jit(solution)/shard_map/dot_general | solution.py:37
  622.7 2.0 fusion.23
  626.4 1.4 reshape.50
  (101 shorter events, 38.3 us)
Async XLA Ops:
  6.5 91.4 %all-reduce.8.cloned.1.call-start = ((), (), s32[]{:S(2)}) async-start(), calls=%async_computation.1 | async-start | bytes 4718592 | tf_op jit(solution)/shard_map/psum | solution.py:9
  29.4 88.8 %slice-start = ((s8[4718592]{0:T(1024)(128)(4,1)}), s8[524288]{0:T(1024)(128)(4,1)S(1)}, s32[]{:S(2)}) async-start(s8[4718592]{0:T(1024)(128)(4,1)} %bitcast.122), calls=%async_computation.2 | async-start | bytes 1048576
  29.4 273.9 %all-reduce.6.cloned.1.call-start = ((), (), s32[]{:S(2)}) async-start(), calls=%async_computation | async-start | bytes 23068672 | tf_op jit(solution)/shard_map/psum | solution.py:30
  97.9 13.7 %copy-start = (f32[576,512]{1,0:T(8,128)S(1)}, f32[576,512]{1,0:T(8,128)}, u32[]{:S(2)}) copy-start(f32[576,512]{1,0:T(8,128)} %get-tuple-element.51) | copy-start | bytes 3538948
  97.9 13.8 %copy-start.1 = (f32[576,512]{1,0:T(8,128)S(1)}, f32[576,512]{1,0:T(8,128)}, u32[]{:S(2)}) copy-start(f32[576,512]{1,0:T(8,128)} %get-tuple-element.52) | copy-start | bytes 3538948
  97.9 20.2 %slice-start.1 = ((s8[4718592]{0:T(1024)(128)(4,1)}), s8[4194304]{0:T(1024)(128)(4,1)S(1)}, s32[]{:S(2)}) async-start(s8[4718592]{0:T(1024)(128)(4,1)} %bitcast.122), calls=%async_computation.3 | async-start | bytes 8388608
  303.4 4.0 copy-start.2
  307.6 1.1 copy-start.6
  448.2 7.5 %copy-start.7 = (f32[4,128,128]{1,2,0:T(8,128)}, f32[4,128,128]{1,2,0:T(8,128)S(1)}, u32[]{:S(2)}) copy-start(f32[4,128,128]{1,2,0:T(8,128)S(1)} %custom-call.34) | copy-start | bytes 786436
  459.4 1.0 copy-start.5
  548.4 52.6 %copy-start.8 = (f32[4,128,128]{1,2,0:T(8,128)S(1)}, f32[4,128,128]{1,2,0:T(8,128)}, u32[]{:S(2)}) copy-start(f32[4,128,128]{1,2,0:T(8,128)} %copy-done.7) | copy-start | bytes 786436
  598.5 3.5 copy-start.4
  605.3 4.2 copy-start.3
Sparse Core Ops, SparseCore 0:
  29.6 68.3 all-reduce.7
  133.9 169.4 all-reduce.5
where the time goes:
time: 641 us; the launch traced here: 635 us
  other arithmetic  258 us (40%)
  waiting for transfers between devices  238 us (37%)
  matrix products  86.7 us (14%)
  local copies, waits for them, and re-layouts  32.3 us (5%)
  between operations  19.4 us (3%)
    psum x1, waiting for transfers between devices, shards(): lax.psum((part_one, part_two, small_one, small_two), 'grp')  170 us
    another operation x5, other arithmetic, solve_lower(): return lax.linalg.triangular_solve(lower, right, left_side=True, lower=True)  80.2 us
    another operation x15, other arithmetic, shards(): jnp.linalg.cholesky(corner_two - jnp.dot(cross.T, cross, precision=highest))  79.6 us
    another operation x14, other arithmetic, shards(): lower_one = jnp.linalg.cholesky(corner_one[:, :width])  79 us
    psum x1, waiting for transfers between devices, from_root(): return lax.psum(kept, axis)  68 us
    another operation x21, matrix products, solve_lower(): return lax.linalg.triangular_solve(lower, right, left_side=True, lower=True)  29.1 us
    another operation x27, local copies, waits for them, and re-layouts, solve_lower(): return lax.linalg.triangular_solve(lower, right, left_side=True, lower=True)  19.9 us
    concatenate x1, other arithmetic, shards(): jnp.concatenate([factor_rows, new_rows], 0).reshape(-1, npanel * width)  15.4 us
  transfers between devices with their start and end apart: 2, of which 2 were waited for; matrix products, arithmetic and copies ran while one was open for 0% of the time, Pallas kernels for 0%

commit v1 on v0

--- a/solution.py
+++ b/solution.py
@@ -6,7 +6,7 @@
 
 def from_root(value, axis, source):
     kept = jnp.where(lax.axis_index(axis) == source, value, 0).astype(value.dtype)
-    return lax.psum(kept, axis)
+    return jnp.sum(lax.all_gather(kept, axis), axis=0)
 
 
 def solve_lower(lower, right):

time: 641 us -> 678 us (1.058)
  waiting for transfers between devices: 238 us -> 252 us
  matrix products: 86.7 us -> 99.5 us
  other arithmetic: 258 us -> 268 us
    all_gather x0 -> x2, waiting for transfers between devices: none -> 83.6 us  [from_root(): return jnp.sum(lax.all_gather(kept, axis), axis=0)]
    psum x1 -> x0, waiting for transfers between devices: 68 us -> none  [from_root(): return lax.psum(kept, axis)]
    dot_general x1, matrix products: 13.7 us -> 24.7 us  [shards(): jnp.dot(second.T, local, precision=highest, preferred_element_type=jnp.fl...]
    reduce_sum x0 -> x2, other arithmetic: none -> 9.9 us  [from_root(): return jnp.sum(lax.all_gather(kept, axis), axis=0)]
  transfers between devices with their start and end apart: 2 -> 3, of which waited for: 2 -> 3; matrix products, arithmetic and copies ran while one was open for 0% -> 4% of each run, Pallas kernels for 0% -> 0%
where the time goes in v1:
time: 678 us; the launch traced here: 671 us
  other arithmetic  268 us (40%)
  waiting for transfers between devices  252 us (37%)
  matrix products  99.5 us (15%)
  local copies, waits for them, and re-layouts  32.6 us (5%)
  between operations  18.8 us (3%)
    psum x1, waiting for transfers between devices, shards(): lax.psum((part_one, part_two, small_one, small_two), 'grp')  168 us
    all_gather x2, waiting for transfers between devices, from_root(): return jnp.sum(lax.all_gather(kept, axis), axis=0)  83.6 us
    another operation x5, other arithmetic, solve_lower(): return lax.linalg.triangular_solve(lower, right, left_side=True, lower=True)  80.4 us
    another operation x15, other arithmetic, shards(): jnp.linalg.cholesky(corner_two - jnp.dot(cross.T, cross, precision=highest))  79.4 us
    another operation x14, other arithmetic, shards(): lower_one = jnp.linalg.cholesky(corner_one[:, :width])  78.9 us
    another operation x21, matrix products, solve_lower(): return lax.linalg.triangular_solve(lower, right, left_side=True, lower=True)  29.1 us
    dot_general x1, matrix products, shards(): jnp.dot(second.T, local, precision=highest, preferred_element_type=jnp.fl...  24.7 us
    another operation x27, local copies, waits for them, and re-layouts, solve_lower(): return lax.linalg.triangular_solve(lower, right, left_side=True, lower=True)  20 us
  transfers between devices with their start and end apart: 3, of which 3 were waited for; matrix products, arithmetic and copies ran while one was open for 4% of the time, Pallas kernels for 0%

profile of v1, /device:TPU:1, one launch (start us, length us, event | category | flops | bytes accessed | tf_op | source)
XLA Modules:
  0.0 671.5 jit_solution(352612033404210304)
XLA Ops:
  6.5 15.4 %maximum_reduce_fusion = f32[576,4,512]{2,1,0:T(4,128)S(1)} fusion(f32[512,4,1,512]{3,2,1,0:T(1,128)} %param.6, f32[64,4,1,512]{3,2,1,0:T(1,128)} %param.5), kind=kLoop, calls=%fused_computation.12 | loop fusion | flops 1179648 | bytes 9437184 | tf_op jit(solution)/shard_map/concatenate | solution.py:21
  22.0 4.4 copy.11
  26.4 3.1 slice_select_fusion.1
  30.3 57.2 %all-gather.7.cloned.1.call-done = f32[4608,512]{1,0:T(8,128)} async-done(((f32[576,512]{1,0:T(8,128)}), f32[4608,512]{1,0:T(8,128)}) %all-gather.7.cloned.1.call-update) | async-done | bytes 9437200 | tf_op jit(solution)/shard_map/all_gather | solution.py:9
  87.5 4.9 reduce_sum.19
  92.5 24.7 %fusion.115 = f32[512,2048]{1,0:T(8,128)} fusion(f32[576,512]{1,0:T(8,128)S(1)} %reduce_sum.19, f32[576,2048]{1,0:T(8,128)} %bitcast.123), kind=kOutput, calls=%fused_computation.189 | convolution fusion | flops 7247757312 | bytes 10092544 | tf_op jit(solution)/shard_map/dot_general | solution.py:26
  117.2 26.4 %all-gather.5.cloned.1.call-done = f32[4608,512]{1,0:T(8,128)} async-done(((f32[576,512]{1,0:T(8,128)}), f32[4608,512]{1,0:T(8,128)}) %all-gather.5.cloned.1.call-update) | async-done | bytes 9437200 | tf_op jit(solution)/shard_map/all_gather | solution.py:9
  143.6 4.9 reduce_sum.18
  148.6 6.5 fusion.29
  155.1 13.6 %fusion.113 = f32[512,2048]{1,0:T(8,128)} fusion(f32[576,512]{1,0:T(8,128)S(1)} %reduce_sum.18, f32[576,2048]{1,0:T(8,128)} %bitcast.124), kind=kOutput, calls=%fused_computation.187 | convolution fusion | flops 7247757312 | bytes 10092544 | tf_op jit(solution)/shard_map/dot_general | solution.py:25
  168.7 3.8 fusion.114
  172.5 167.9 %all-reduce.4.cloned.1.call-done = (f32[512,2048]{1,0:T(8,128)}, f32[512,2048]{1,0:T(8,128)}, f32[512,1024]{0,1:T(8,128)}, f32[512,512]{0,1:T(8,128)}) async-done(((f32[512,2048]{1,0:T(8,128)}, f32[512,2048]{1,0:T(8,128)}, f32[512,1024]{0,1:T(8,128)}, f32[512,512]{0,1:T(8,128)}), (f32[512,2048]{1,0:T(8,128)}, f32[512,2048]{1,0:T(8,128)}, f32[512,1024]{0,1:T(8,128)}, ...) | async-done | bytes 11534352 | tf_op jit(solution)/shard_map/psum | solution.py:30
  340.4 2.5 slice.184
  342.9 1.6 copy.4
  345.8 11.7 %cholesky.286 = f32[128,128]{1,0:T(8,128)S(1)} custom-call(f32[128,128]{1,0:T(8,128)S(1)} %cholesky.426), custom_call_target="Cholesky" | custom-call | tf_op jit(solution)/shard_map/jit(cholesky)/cholesky | solution.py:33
  357.5 9.8 %custom-call.31 = f32[1,128,128]{1,2,0:T(8,128)S(1)} custom-call(f32[1,128,128]{2,1,0:T(8,128)S(1)} %get-tuple-element.76), custom_call_target="InvertDiagBlocksLowerTriangular" | custom-call | tf_op jit(solution)/shard_map/jit(cholesky)/cholesky | solution.py:33
  370.0 11.9 %cholesky.305 = f32[128,128]{1,0:T(8,128)S(1)} custom-call(f32[128,128]{1,0:T(8,128)S(1)} %cholesky.430), custom_call_target="Cholesky" | custom-call | tf_op jit(solution)/shard_map/jit(cholesky)/cholesky | solution.py:33
  381.9 9.8 %custom-call.32 = f32[1,128,128]{1,2,0:T(8,128)S(1)} custom-call(f32[1,128,128]{2,1,0:T(8,128)S(1)} %get-tuple-element.73), custom_call_target="InvertDiagBlocksLowerTriangular" | custom-call | tf_op jit(solution)/shard_map/jit(cholesky)/cholesky | solution.py:33
  393.3 11.7 %cholesky.326 = f32[128,128]{1,0:T(8,128)S(1)} custom-call(f32[128,128]{1,0:T(8,128)S(1)} %cholesky.435), custom_call_target="Cholesky" | custom-call | tf_op jit(solution)/shard_map/jit(cholesky)/cholesky | solution.py:33
  405.7 9.8 %custom-call.33 = f32[1,128,128]{1,2,0:T(8,128)S(1)} custom-call(f32[1,128,128]{2,1,0:T(8,128)S(1)} %get-tuple-element.70), custom_call_target="InvertDiagBlocksLowerTriangular" | custom-call | tf_op jit(solution)/shard_map/jit(cholesky)/cholesky | solution.py:33
  417.0 12.1 %cholesky.343 = f32[128,128]{1,0:T(8,128)S(1)} custom-call(f32[128,128]{1,0:T(8,128)S(1)} %convolution_subtract_fusion.13), custom_call_target="Cholesky" | custom-call | tf_op jit(solution)/shard_map/jit(cholesky)/cholesky | solution.py:33
  434.0 11.9 %while.5 = (s32[]{:T(128)}, f32[512,512]{1,0:T(8,128)}, s32[4,2]{0,1:T(2,128)S(1)}, f32[4,128,128]{2,1,0:T(8,128)S(1)}, s32[]{:T(128)}) while((s32[]{:T(128)}, f32[512,512]{1,0:T(8,128)}, s32[4,2]{0,1:T(2,128)S(1)}, f32[4,128,128]{2,1,0:T(8,128)S(1)}, s32[]{:T(128)}) %tuple.55), condition=%wide.while_cond, body=%wide.while_body.sunk | while | flops 2 | bytes 131181 | solution.py:13
  434.7 2.3 bitcast_dynamic-update-slice_fusion.4
  437.6 2.3 bitcast_dynamic-update-slice_fusion.4
  440.6 2.3 bitcast_dynamic-update-slice_fusion.4
  443.6 2.2 bitcast_dynamic-update-slice_fusion.4
  445.9 39.3 %custom-call.34 = f32[4,128,128]{1,2,0:T(8,128)S(1)} custom-call(f32[4,128,128]{2,1,0:T(8,128)S(1)} %get-tuple-element.29), custom_call_target="InvertDiagBlocksLowerTriangular" | custom-call | tf_op jit(solution)/shard_map/triangular_solve/custom-call.3 | solution.py:13
  485.6 1.4 convolution_subtract_fusion.6
  487.5 1.9 convolution_subtract_fusion.5
  489.8 2.4 convolution_subtract_fusion.7
  492.7 3.1 convolution_subtract_fusion.4
  497.3 11.7 %cholesky.358 = f32[128,128]{1,0:T(8,128)S(1)} custom-call(f32[128,128]{1,0:T(8,128)S(1)} %cholesky.439), custom_call_target="Cholesky" | custom-call | tf_op jit(solution)/shard_map/jit(cholesky)/cholesky | solution.py:35
  509.2 10.0 %custom-call.35 = f32[1,128,128]{1,2,0:T(8,128)S(1)} custom-call(f32[1,128,128]{2,1,0:T(8,128)S(1)} %get-tuple-element.66), custom_call_target="InvertDiagBlocksLowerTriangular" | custom-call | tf_op jit(solution)/shard_map/jit(cholesky)/cholesky | solution.py:35
  521.7 11.7 %cholesky.377 = f32[128,128]{1,0:T(8,128)S(1)} custom-call(f32[128,128]{1,0:T(8,128)S(1)} %cholesky.443), custom_call_target="Cholesky" | custom-call | tf_op jit(solution)/shard_map/jit(cholesky)/cholesky | solution.py:35
  534.7 9.8 %custom-call.36 = f32[1,128,128]{1,2,0:T(8,128)S(1)} custom-call(f32[1,128,128]{2,1,0:T(8,128)S(1)} %get-tuple-element.63), custom_call_target="InvertDiagBlocksLowerTriangular" | custom-call | tf_op jit(solution)/shard_map/jit(cholesky)/cholesky | solution.py:35
  546.1 11.7 %cholesky.398 = f32[128,128]{1,0:T(8,128)S(1)} custom-call(f32[128,128]{1,0:T(8,128)S(1)} %cholesky.448), custom_call_target="Cholesky" | custom-call | tf_op jit(solution)/shard_map/jit(cholesky)/cholesky | solution.py:35
  558.6 10.0 %custom-call.37 = f32[1,128,128]{1,2,0:T(8,128)S(1)} custom-call(f32[1,128,128]{2,1,0:T(8,128)S(1)} %get-tuple-element.60), custom_call_target="InvertDiagBlocksLowerTriangular" | custom-call | tf_op jit(solution)/shard_map/jit(cholesky)/cholesky | solution.py:35
  570.0 11.7 %cholesky.415 = f32[128,128]{1,0:T(8,128)S(1)} custom-call(f32[128,128]{1,0:T(8,128)S(1)} %convolution_subtract_fusion.12), custom_call_target="Cholesky" | custom-call | tf_op jit(solution)/shard_map/jit(cholesky)/cholesky | solution.py:35
  585.2 8.3 %while.6 = (s32[]{:T(128)}, f32[512,512]{1,0:T(8,128)S(1)}, s32[4,2]{0,1:T(2,128)S(1)}, f32[4,128,128]{2,1,0:T(8,128)S(1)}, s32[]{:T(128)}) while((s32[]{:T(128)}, f32[512,512]{1,0:T(8,128)S(1)}, s32[4,2]{0,1:T(2,128)S(1)}, f32[4,128,128]{2,1,0:T(8,128)S(1)}, s32[]{:T(128)}) %tuple.68), condition=%wide.while_cond.clone, body=%wide.while_body.clone.sunk | while | flops 2 | bytes 131181 | solution.py:13
  592.1 1.4 bitcast_dynamic-update-slice_fusion.5
  593.5 39.7 %custom-call.38 = f32[4,128,128]{1,2,0:T(8,128)S(1)} custom-call(f32[4,128,128]{2,1,0:T(8,128)S(1)} %get-tuple-element.30), custom_call_target="InvertDiagBlocksLowerTriangular" | custom-call | tf_op jit(solution)/shard_map/triangular_solve/custom-call.3 | solution.py:13
  633.2 2.3 fusion.41
  635.5 2.4 convolution_subtract_fusion.3
  639.0 2.2 convolution_subtract_fusion.1
  642.3 3.1 fusion.26
  646.5 7.7 %fusion.20 = f32[512,2048]{1,0:T(8,128)S(1)} fusion(f32[512,2048]{1,0:T(8,128)S(1)} %copy-done.1, f32[128,2048]{1,0:T(8,128)S(1)} %fusion.99, f32[128,2048]{1,0:T(8,128)S(1)} %fusion.97, f32[128,2048]{1,0:T(8,128)S(1)} %fusion.95, f32[128,2048]{1,0:T(8,128)S(1)} %fusion.41, f32[128,512]{1,0:T(8,128)S(1)} %fusion.98, f32[128,512]{1,0:T(8,128)S(1)} %fusion.96, ...), kind=kOutput, calls=%fused_computation.33 | convolution fusion | flops 6447431680 | bytes 13631488 | tf_op jit(solution)/shard_map/dot_general | solution.py:37
  659.7 2.0 fusion.23
  663.3 1.4 reshape.50
  (97 shorter events, 42.6 us)
Async XLA Ops:
  6.5 81.0 %all-gather.7.cloned.1.call-start = ((), (), s32[]{:S(2)}) async-start(), calls=%async_computation.1 | async-start | bytes 10616832 | tf_op jit(solution)/shard_map/all_gather | solution.py:9
  29.5 114.1 %all-gather.5.cloned.1.call-start = ((), (), s32[]{:S(2)}) async-start(), calls=%async_computation | async-start | bytes 10616832 | tf_op jit(solution)/shard_map/all_gather | solution.py:9
  30.2 310.1 %all-reduce.4.cloned.1.call-start = ((), (), s32[]{:S(2)}) async-start(), calls=%async_computation.2 | async-start | bytes 23068672 | tf_op jit(solution)/shard_map/psum | solution.py:30
  340.4 4.1 copy-start
  344.7 1.1 copy-start.4
  485.2 7.5 %copy-start.5 = (f32[4,128,128]{1,2,0:T(8,128)}, f32[4,128,128]{1,2,0:T(8,128)S(1)}, u32[]{:S(2)}) copy-start(f32[4,128,128]{1,2,0:T(8,128)S(1)} %custom-call.34) | copy-start | bytes 786436
  496.3 1.0 copy-start.3
  585.1 52.8 %copy-start.6 = (f32[4,128,128]{1,2,0:T(8,128)S(1)}, f32[4,128,128]{1,2,0:T(8,128)}, u32[]{:S(2)}) copy-start(f32[4,128,128]{1,2,0:T(8,128)} %copy-done.5) | copy-start | bytes 786436
  635.5 3.5 copy-start.2
  642.3 4.2 copy-start.1
Sparse Core Ops, SparseCore 0:
  29.6 57.8 all-gather.6
  89.2 54.3 all-gather.4
  172.6 167.7 all-reduce.3
